TPU v7x, 256 devices: a whole 4x4x8 slice. The times are simulated.
256 devices in a mesh: tm: 64 (over z, x_hi, y), chan: 4 (over x_lo, core).
Axes of the slice: x: 4 (x_hi: 2, x_lo: 2; x = x_hi * 2 + x_lo), y: 4, z: 8, core: 2. Of those that a mesh axis runs over, the one named last changes fastest.
Arguments:
- signal: float32 [256, 8192], P('chan', 'tm'), may hold values from -256 to 256
- support: int32 [32], replicated, may hold values from 1 to 4, as said below
- pair_first: int32 [4, 512], replicated, may hold values from 0 to 255
- pair_second: int32 [4, 512], replicated, may hold values from 0 to 255
- pair_count: int32 [4], replicated, may hold values from 128 to 512, as said below
Outputs:
- cross: float32 [4, 512, 2, 32], P('chan', 'tm')
- coherence: float32 [4, 512, 32], P('chan', 'tm')
Inputs may be any that keep to these rules, and one draw needn't show every extreme that they name: With b = q // 8 the band of scale q, support[q] is at most (4 * 128 / 4^(3 - b) + 127) // 128, and equals it for the last scale of every band. The live slots of an owner are its first pair_count slots; some owner has all 512 slots live.
All inputs are finite; a program needn't handle non-finite values.
Results may differ from a plain program's by a relative error of at most 0.0027.
Values may be sent and summed in bfloat16 or wider, within the bound.
No kernel may reach another device: no remote copies, remote signals or barrier semaphores. Data moves between devices by JAX's collectives and lax.ppermute only.
A program may use at most 192 MiB of HBM per device.

v0:
```python
import math
import jax
import jax.numpy as jnp
import numpy as np
from jax import lax
from jax.sharding import PartitionSpec as P

NS = 32
BLK = 128
TD = 128
power_floor = 1e-06


def from_behind(array, axis, by):
    peers = lax.axis_size(axis)
    return lax.ppermute(array, axis, [(i, (i + by) % peers) for i in range(peers)])


def morlet_parts(offset, scale_index, reach_blocks):
    scale_width = 2.0 * TD * jnp.exp2((scale_index - (NS - 1)).astype(jnp.float32) / 4.0)
    scaled_offset = offset.astype(jnp.float32) / scale_width
    amplitude = (
        math.pi ** (-0.25) * lax.rsqrt(scale_width) * jnp.exp(-0.5 * scaled_offset * scaled_offset)
    )
    inside = jnp.abs(offset) < reach_blocks * BLK
    real_part = jnp.where(inside, amplitude * jnp.cos(6.0 * scaled_offset), 0.0)
    imag_part = jnp.where(inside, amplitude * jnp.sin(6.0 * scaled_offset), 0.0)
    return (real_part.astype(jnp.bfloat16), imag_part.astype(jnp.bfloat16))


def wavelet_band(extended, scale_ids, reaches, offsets, time_span):
    channels = extended.shape[0]
    blocks = time_span // BLK
    centre = 4 * time_span // BLK
    tap_blocks = 2 * offsets + 1
    pieces = [
        extended[:, (centre + offset_step) * BLK : (centre + offset_step) * BLK + time_span]
        for offset_step in range(-offsets, offsets + 1)
    ]
    unfolded = jnp.stack(pieces, axis=1).reshape(channels, tap_blocks, blocks, BLK)
    unfolded = unfolded.transpose(0, 2, 1, 3).reshape(channels * blocks, tap_blocks * BLK)
    lag_start = (jnp.arange(tap_blocks, dtype=jnp.int32) - offsets) * BLK
    within = jnp.arange(BLK, dtype=jnp.int32)
    tap_offset = lag_start[:, None, None] + within[None, :, None] - within[None, None, :]

    def single_scale(scale_index, reach_blocks):
        return morlet_parts(tap_offset, scale_index, reach_blocks)

    real_part, imag_part = jax.vmap(single_scale)(scale_ids, reaches)
    kernel_table = jnp.stack([real_part, imag_part], axis=1)
    kernel_table = kernel_table.transpose(2, 3, 0, 1, 4).reshape(tap_blocks * BLK, -1)
    coefficients = jnp.dot(unfolded, kernel_table, preferred_element_type=jnp.float32)
    scale_count = scale_ids.shape[0]
    coefficients = coefficients.astype(jnp.bfloat16).reshape(channels, blocks, scale_count, 2, BLK)
    return coefficients.transpose(2, 3, 0, 1, 4).reshape(scale_count, 2 * channels, time_span)


def pair_spectra(coefficients, flat_index):
    channels = coefficients.shape[1] // 2
    scale_count = coefficients.shape[0]
    gram_matrix = jnp.einsum(
        "qat,qbt->qab", coefficients, coefficients, preferred_element_type=jnp.float32
    )
    real_part = gram_matrix[:, :channels, :channels] + gram_matrix[:, channels:, channels:]
    imag_part = gram_matrix[:, channels:, :channels] - gram_matrix[:, :channels, channels:]
    auto_power = jnp.diagonal(real_part, axis1=1, axis2=2)
    real_pairs = jnp.take(real_part.reshape(scale_count, -1), flat_index, axis=1)
    imag_pairs = jnp.take(imag_part.reshape(scale_count, -1), flat_index, axis=1)
    return (real_pairs, imag_pairs, auto_power)


def shards(signal, support, pair_first, pair_second, pair_count):
    groups = lax.axis_size("chan")
    cluster_number = lax.axis_index("chan")
    time_index = lax.axis_index("tm")
    time_devices = lax.axis_size("tm")
    time_span = signal.shape[1]
    ntime = time_span * time_devices
    rounded = signal.astype(jnp.bfloat16)
    gathered = lax.all_gather(rounded, "chan", axis=0, tiled=True)
    neighbours = [
        from_behind(gathered, "tm", distance) for distance in (4, 3, 2, 1, -1, -2, -3, -4)
    ]
    extended = jnp.concatenate(neighbours[:4] + [gathered] + neighbours[4:], axis=1)
    channels = extended.shape[0]
    first_flat = pair_first.reshape(-1)
    second_flat = pair_second.reshape(-1)
    flat_index = first_flat * channels + second_flat
    per_group = NS // groups
    scale_ids = cluster_number * per_group + jnp.arange(per_group, dtype=jnp.int32)
    coefficients = wavelet_band(
        extended, scale_ids, support[scale_ids], 4 * time_span // BLK, time_span
    )
    real_pairs, imag_pairs, auto_power = pair_spectra(coefficients, flat_index)
    position = np.arange(NS)
    owner_devices = pair_first.shape[0]
    slots_total = pair_first.shape[1]
    stacked = jnp.stack([real_pairs, imag_pairs], axis=0)
    columns = stacked.shape[0]
    partial_value = stacked.reshape(columns, per_group, owner_devices, slots_total).transpose(
        2, 3, 0, 1
    )
    summed = lax.psum_scatter(partial_value, "tm", scatter_dimension=1, tiled=True)
    owned = lax.all_to_all(summed, "chan", split_axis=0, concat_axis=3, tiled=True)
    owned = owned[:, :, :, position] / ntime
    slots_local = owned.shape[1]
    slot_index = time_index * slots_local + jnp.arange(slots_local, dtype=jnp.int32)
    alive_mask = slot_index < pair_count[cluster_number]
    cross_real = owned[0, :, 0, :]
    cross_imag = owned[0, :, 1, :]
    power_total = lax.psum(auto_power, "tm")
    power_groups = lax.all_gather(power_total, "chan", axis=0, tiled=True)
    power_all = power_groups[position] / ntime
    first_row = lax.dynamic_index_in_dim(pair_first, cluster_number, 0, False)
    second_row = lax.dynamic_index_in_dim(pair_second, cluster_number, 0, False)
    first_owned = lax.dynamic_slice_in_dim(first_row, time_index * slots_local, slots_local)
    second_owned = lax.dynamic_slice_in_dim(second_row, time_index * slots_local, slots_local)
    first_power = power_all[:, first_owned].T
    second_power = power_all[:, second_owned].T
    coherence = (cross_real * cross_real + cross_imag * cross_imag) / (
        (first_power + power_floor) * (second_power + power_floor)
    )
    coherence = jnp.where(alive_mask[:, None], coherence, 0.0)[None]
    cross = jnp.stack([cross_real, cross_imag], axis=1)
    cross = jnp.where(alive_mask[:, None, None], cross, 0.0)[None]
    return (cross, coherence.astype(jnp.float32))


def solution(mesh):
    in_specs = (P("chan", "tm"), P(), P(), P(), P())
    out_specs = (P("chan", "tm", None, None), P("chan", "tm", None))
    return jax.shard_map(shards, mesh=mesh, in_specs=in_specs, out_specs=out_specs, check_vma=False)
```

profile of v0, /device:TPU:1, one launch (start us, length us, event | category | flops | bytes accessed | tf_op | source)
XLA Modules:
  0.0 1023.3 jit_solution(1796853218506428714)
XLA Ops:
  7.2 0.8 convert_element_type.43
  8.0 8.3 all_gather.6
  16.4 6.4 collective-permute-start.7
  22.8 1.2 collective-permute-start.6
  24.0 5.5 collective-permute-start.5
  29.5 1.1 collective-permute-start.4
  30.7 0.8 fusion.11
  31.4 0.8 fusion.12
  32.2 0.7 add_bitcast_fusion
  32.9 1.2 dynamic_slice.16
  34.2 0.6 gather_fusion
  35.2 147.0 %fusion.2 = (bf16[8,1,9,128,128]{4,1,0,3,2:T(2,128)(2,1)S(1)}, bf16[8,1,9,128,128]{4,1,0,3,2:T(2,128)(2,1)S(1)}) fusion(s32[9,128,128]{2,1,0:T(8,128)S(1)} %get-tuple-element.16, s32[8]{0:T(128)S(1)} %broadcast_multiply_fusion.1, f32[8]{0:T(128)S(1)} %get-tuple-element.20, f32[9,128,128]{2,1,0:T(8,128)S(1)} %get-tuple-element.15, f32[8]{0:T(128)S(1)} %get-tuple-element.19), kind=kLoop, calls=%fused_computation.13 | loop fusion | flops 14155776 | bytes 5898336 | tf_op jit(solution)/shard_map/vmap()/convert_element_type | solution.py:28
  182.2 11.7 %maximum_bitcast_fusion = bf16[9,128,8,2,128]{4,3,2,1,0:T(2,128)(2,1)} fusion(bf16[8,1,9,128,128]{4,1,0,3,2:T(2,128)(2,1)S(1)} %get-tuple-element.14, bf16[8,1,9,128,128]{4,1,0,3,2:T(2,128)(2,1)S(1)} %get-tuple-element.13), kind=kLoop, calls=%fused_computation.15 | loop fusion | flops 9437184 | bytes 9437184 | tf_op jit(solution)/shard_map/transpose | solution.py:51
  193.9 8.8 reshape.232
  202.8 0.6 dynamic-slice.2
  204.2 7.6 collective-permute-done.1
  211.8 9.1 collective-permute-done.2
  220.9 0.4 collective-permute-start.3
  221.3 8.4 collective-permute-done.3
  229.9 3.9 convolution_convert_fusion
  233.7 0.8 reshape.233
  234.8 1.3 fusion.13
  236.0 1.9 slice_add_fusion
  237.9 17.3 %copy.84 = f32[8,256,256]{0,2,1:T(8,128)} copy(f32[8,256,256]{2,1,0:T(8,128)} %get-tuple-element.11) | data formatting | bytes 4194304 | tf_op jit(solution)/shard_map/reshape | solution.py:67
  255.2 16.2 %copy.85 = f32[8,256,256]{0,2,1:T(8,128)} copy(f32[8,256,256]{2,1,0:T(8,128)S(1)} %get-tuple-element.12) | data formatting | bytes 4194304 | tf_op jit(solution)/shard_map/reshape | solution.py:68
  271.4 16.0 %gather_fusion.6 = f32[2048,8]{1,0:T(8,128)S(1)} fusion(f32[8,65536]{0,1:T(8,128)} %bitcast.81, s32[2048]{0:T(1024)S(1)} %fusion.9), kind=kCustom, calls=%fused_computation.clone | custom fusion | bytes 139264 | tf_op jit(solution)/shard_map/jit(_take)/gather | solution.py:67
  287.4 16.0 %gather_fusion.7 = f32[2048,8]{1,0:T(8,128)S(1)} fusion(f32[8,65536]{0,1:T(8,128)} %bitcast.82, s32[2048]{0:T(1024)S(1)} %fusion.9), kind=kCustom, calls=%fused_computation.1.clone | custom fusion | bytes 139264 | tf_op jit(solution)/shard_map/jit(_take)/gather | solution.py:68
  303.4 0.3 broadcast_select_fusion.1
  303.8 0.7 copy.71
  304.5 0.7 copy.72
  305.1 1.9 maximum_bitcast_fusion.1
  307.1 0.7 add_compare_fusion
  307.8 2.3 gather_fusion.2
  310.1 299.8 %psum.7 = f32[8,256]{0,1:T(8,128)S(1)} all-reduce(f32[8,256]{0,1:T(8,128)S(1)} %bitcast.88), channel_id=1, replica_groups=mesh['tm'=64,'chan'=4] {'tm'}, use_global_device_ids=true, to_apply=%region_1.3 | all-reduce | flops 2048 | bytes 16384 | tf_op jit(solution)/shard_map/psum | solution.py:111
  609.9 61.3 %all_gather.7 = f32[32,256]{1,0:T(8,128)S(1)} all-gather(f32[8,256]{1,0:T(8,128)S(1)} %copy.77), channel_id=1, replica_groups=mesh['tm'=64,'chan'=4] {'chan'}, dimensions={0}, use_global_device_ids=true | all-gather | bytes 40960 | tf_op jit(solution)/shard_map/all_gather | solution.py:112
  671.2 0.6 gather_fusion.3
  671.8 287.3 %all-reduce.3.cloned.1.call-done = f32[4,512,2,8]{3,0,1,2:T(4,128)} async-done(((f32[4,512,2,8]{3,0,1,2:T(4,128)}), f32[4,512,2,8]{3,0,1,2:T(4,128)}) %all-reduce.3.cloned.1.call-update) | async-done | bytes 131088
  959.0 0.8 constant_dynamic-slice_fusion
  959.8 0.7 reshape.313
  960.5 49.6 %all-to-all-start = ((f32[4,1,128]{2,1,0:T(1,128)}), f32[4,1,128]{2,1,0:T(1,128)S(1)}, u32[]{:S(2)}, u32[]{:S(2)}) async-start(f32[4,1,128]{2,1,0:T(1,128)} %reshape.313), calls=%async_computation | async-start | bytes 4096 | tf_op jit(solution)/shard_map/all_to_all | solution.py:104
  1010.2 0.6 gather_fusion.5
  1010.7 0.6 gather_fusion.4
  1011.4 1.6 all-to-all-done
  1013.0 0.5 broadcast.405
  1013.5 0.7 reduce
  1014.4 0.6 gather_fusion.1
  1015.1 0.7 copy.82
  1015.8 0.7 copy.83
  (54 shorter events, 1.6 us)
Async XLA Ops:
  7.2 27.0 %copy-start = (s32[32]{0:T(128)S(1)}, s32[32]{0:T(128)}, u32[]{:S(2)}) copy-start(s32[32]{0:T(128)} %param.11) | copy-start | bytes 388
  7.2 951.8 %all-reduce.3.cloned.1.call-start = ((), (), s32[]{:S(2)}) async-start(), calls=%async_computation.1 | async-start | bytes 4194304
  16.4 213.4 %collective-permute-start.7 = (bf16[256,128]{0,1:T(8,128)(2,1)S(1)}, bf16[256,128]{0,1:T(8,128)(2,1)S(1)}, u32[]{:S(2)}, u32[]{:S(2)}) collective-permute-start(bf16[256,128]{0,1:T(8,128)(2,1)S(1)} %copy.59), channel_id=1, source_target_pairs={{0,240},{4,244},{8,248},{12,252},{16,0},{20,4},{24,8},{28,12},{32,... | collective-permute-start | bytes 196616 | tf_op jit(solution)/shard_map/ppermute | solution.py:16
  22.8 207.0 %collective-permute-start.6 = (bf16[256,128]{0,1:T(8,128)(2,1)S(1)}, bf16[256,128]{0,1:T(8,128)(2,1)S(1)}, u32[]{:S(2)}, u32[]{:S(2)}) collective-permute-start(bf16[256,128]{0,1:T(8,128)(2,1)S(1)} %copy.59), channel_id=1, source_target_pairs={{0,244},{4,248},{8,252},{12,0},{16,4},{20,8},{24,12},{28,16},{32,2... | collective-permute-start | bytes 196616 | tf_op jit(solution)/shard_map/ppermute | solution.py:16
  24.0 205.8 %collective-permute-start.5 = (bf16[256,128]{0,1:T(8,128)(2,1)S(1)}, bf16[256,128]{0,1:T(8,128)(2,1)S(1)}, u32[]{:S(2)}, u32[]{:S(2)}) collective-permute-start(bf16[256,128]{0,1:T(8,128)(2,1)S(1)} %copy.59), channel_id=1, source_target_pairs={{0,248},{4,252},{8,0},{12,4},{16,8},{20,12},{24,16},{28,20},{32,24... | collective-permute-start | bytes 196616 | tf_op jit(solution)/shard_map/ppermute | solution.py:16
  29.5 200.2 %collective-permute-start.4 = (bf16[256,128]{0,1:T(8,128)(2,1)S(1)}, bf16[256,128]{0,1:T(8,128)(2,1)S(1)}, u32[]{:S(2)}, u32[]{:S(2)}) collective-permute-start(bf16[256,128]{0,1:T(8,128)(2,1)S(1)} %copy.59), channel_id=1, source_target_pairs={{0,252},{4,0},{8,4},{12,8},{16,12},{20,16},{24,20},{28,24},{32,28}... | collective-permute-start | bytes 196616 | tf_op jit(solution)/shard_map/ppermute | solution.py:16
  30.6 173.4 %collective-permute-start = (bf16[256,128]{0,1:T(8,128)(2,1)S(1)}, bf16[256,128]{0,1:T(8,128)(2,1)S(1)}, u32[]{:S(2)}, u32[]{:S(2)}) collective-permute-start(bf16[256,128]{0,1:T(8,128)(2,1)S(1)} %copy.59), channel_id=1, source_target_pairs={{0,16},{4,20},{8,24},{12,28},{16,32},{20,36},{24,40},{28,44},{32,4... | collective-permute-start | bytes 196616 | tf_op jit(solution)/shard_map/ppermute | solution.py:16
  193.9 8.9 copy-start.2
  204.1 7.7 collective-permute-start.1
  211.8 9.1 collective-permute-start.2
  220.9 8.8 collective-permute-start.3
  304.4 712.0 %copy-start.1 = (s32[32]{0:T(128)S(1)}, s32[32]{0:T(128)}, u32[]{:S(2)}) copy-start(s32[32]{0:T(128)} %param.11) | copy-start | bytes 388
  960.5 52.6 %all-to-all-start = ((f32[4,1,128]{2,1,0:T(1,128)}), f32[4,1,128]{2,1,0:T(1,128)S(1)}, u32[]{:S(2)}, u32[]{:S(2)}) async-start(f32[4,1,128]{2,1,0:T(1,128)} %reshape.313), calls=%async_computation | async-start | bytes 4096 | tf_op jit(solution)/shard_map/all_to_all | solution.py:104
Sparse Core Ops, SparseCore 0:
  307.2 651.7 all-reduce.2
where the time goes:
time: 1020 us
  blocking collectives  369 us (36%)
  waiting for transfers between devices  314 us (31%)
  other arithmetic  168 us (16%)
  local copies, waits for them, and re-layouts  87.8 us (9%)
  starting transfers between devices  64.3 us (6%)
  between operations  15 us (1%)
    psum x1, blocking collectives, shards(): power_total = lax.psum(auto_power, 'tm')  300 us
    unnamed x2, waiting for transfers between devices  287 us
    convert_element_type x1, other arithmetic, morlet_parts(): return (real_part.astype(jnp.bfloat16), imag_part.astype(jnp.bfloat16))  147 us
    all_gather x1, blocking collectives, shards(): power_groups = lax.all_gather(power_total, 'chan', axis=0, tiled=True)  61.3 us
    all_to_all x1, starting transfers between devices, shards(): lax.all_to_all(summed, 'chan', split_axis=0, concat_axis=3, tiled=True)  49.6 us
    ppermute x8, waiting for transfers between devices, from_behind(): lax.ppermute(array, axis, [(i, (i + by) % peers) for i in range(peers)])  25.2 us
  transfers between devices with their start and end apart: 10, of which 5 were waited for; matrix products, arithmetic and copies ran while one was open for 17% of the time, Pallas kernels for 0%

commit v1 on v0

--- a/solution.py
+++ b/solution.py
@@ -101,7 +101,10 @@
         2, 3, 0, 1
     )
     summed = lax.psum_scatter(partial_value, "tm", scatter_dimension=1, tiled=True)
-    owned = lax.all_to_all(summed, "chan", split_axis=0, concat_axis=3, tiled=True)
+    owned = jnp.concatenate(
+        lax.all_to_all(jnp.stack(jnp.split(summed, lax.axis_size("chan"), axis=0)), "chan", 0, 0),
+        axis=3,
+    )
     owned = owned[:, :, :, position] / ntime
     slots_local = owned.shape[1]
     slot_index = time_index * slots_local + jnp.arange(slots_local, dtype=jnp.int32)

time: 1020 us -> 688 us (0.67)
  waiting for transfers between devices: 314 us -> 26.8 us
  starting transfers between devices: 64.3 us -> 18 us
    unnamed x2 -> x1, waiting for transfers between devices: 287 us -> 0.02 us
    all_to_all x1, starting transfers between devices: 49.6 us -> 3.38 us  [shards(): lax.all_to_all(jnp.stack(jnp.split(summed, lax.axis_size('chan'), axis=0)...]
  transfers between devices with their start and end apart: 10 -> 10, of which waited for: 5 -> 4; matrix products, arithmetic and copies ran while one was open for 17% -> 26% of each run, Pallas kernels for 0% -> 0%
where the time goes in v1:
time: 688 us; the launch traced here: 687 us
  blocking collectives  369 us (54%)
  other arithmetic  167 us (24%)
  local copies, waits for them, and re-layouts  85.8 us (12%)
  waiting for transfers between devices  26.8 us (4%)
  starting transfers between devices  18 us (3%)
  between operations  14.3 us (2%)
    psum x1, blocking collectives, shards(): power_total = lax.psum(auto_power, 'tm')  302 us
    convert_element_type x1, other arithmetic, morlet_parts(): return (real_part.astype(jnp.bfloat16), imag_part.astype(jnp.bfloat16))  147 us
    all_gather x1, blocking collectives, shards(): power_groups = lax.all_gather(power_total, 'chan', axis=0, tiled=True)  59.1 us
    ppermute x8, waiting for transfers between devices, from_behind(): lax.ppermute(array, axis, [(i, (i + by) % peers) for i in range(peers)])  25.2 us
    reshape x1, local copies, waits for them, and re-layouts, pair_spectra(): real_part.reshape(scale_count, -1)  17.3 us
    reshape x1, local copies, waits for them, and re-layouts, pair_spectra(): imag_part.reshape(scale_count, -1)  16.2 us
    gather x1, local copies, waits for them, and re-layouts, pair_spectra(): jnp.take(imag_part.reshape(scale_count, -1), flat_index, axis=1)  16 us
    gather x1, local copies, waits for them, and re-layouts, pair_spectra(): jnp.take(real_part.reshape(scale_count, -1), flat_index, axis=1)  16 us
  transfers between devices with their start and end apart: 10, of which 4 were waited for; matrix products, arithmetic and copies ran while one was open for 26% of the time, Pallas kernels for 0%

profile of v1, /device:TPU:1, one launch (start us, length us, event | category | flops | bytes accessed | tf_op | source)
XLA Modules:
  0.0 686.8 jit_solution(315308960189223498)
XLA Ops:
  7.2 0.8 convert_element_type.43
  8.0 8.3 %all_gather.6 = bf16[256,128]{1,0:T(8,128)(2,1)S(1)} all-gather(bf16[64,128]{1,0:T(8,128)(2,1)S(1)} %convert_element_type.43), channel_id=1, replica_groups=mesh['tm'=64,'chan'=4] {'chan'}, dimensions={0}, use_global_device_ids=true | all-gather | bytes 81920 | tf_op jit(solution)/shard_map/all_gather | solution.py:80
  16.3 0.1 copy.61
  16.4 6.4 collective-permute-start.7
  22.8 1.2 collective-permute-start.6
  24.0 5.5 collective-permute-start.5
  29.5 1.1 collective-permute-start.4
  30.7 0.7 add_bitcast_fusion
  31.4 1.2 dynamic_slice.16
  32.7 0.6 gather_fusion
  33.4 0.2 fusion.4
  33.6 147.0 %fusion.2 = (bf16[8,1,9,128,128]{4,1,0,3,2:T(2,128)(2,1)S(1)}, bf16[8,1,9,128,128]{4,1,0,3,2:T(2,128)(2,1)S(1)}) fusion(s32[9,128,128]{2,1,0:T(8,128)S(1)} %get-tuple-element.20, s32[8]{0:T(128)S(1)} %broadcast_multiply_fusion.1, f32[8]{0:T(128)S(1)} %get-tuple-element.24, f32[9,128,128]{2,1,0:T(8,128)S(1)} %get-tuple-element.19, f32[8]{0:T(128)S(1)} %get-tuple-element.23), kind=kLoop, calls=%fused_computation.13 | loop fusion | flops 14155776 | bytes 5898336 | tf_op jit(solution)/shard_map/vmap()/convert_element_type | solution.py:28
  180.7 11.7 %maximum_bitcast_fusion = bf16[9,128,8,2,128]{4,3,2,1,0:T(2,128)(2,1)} fusion(bf16[8,1,9,128,128]{4,1,0,3,2:T(2,128)(2,1)S(1)} %get-tuple-element.14, bf16[8,1,9,128,128]{4,1,0,3,2:T(2,128)(2,1)S(1)} %get-tuple-element.13), kind=kLoop, calls=%fused_computation.15 | loop fusion | flops 9437184 | bytes 9437184 | tf_op jit(solution)/shard_map/transpose | solution.py:51
  192.4 8.8 %reshape.238 = bf16[1152,2048]{1,0:T(8,128)(2,1)} reshape(bf16[9,128,8,2,128]{4,3,2,1,0:T(2,128)(2,1)} %maximum_bitcast_fusion) | data formatting | bytes 9437184 | tf_op jit(solution)/shard_map/reshape | solution.py:51
  201.2 0.8 fusion.11
  202.0 0.8 fusion.12
  202.8 7.6 %collective-permute-done.1 = bf16[256,128]{0,1:T(8,128)(2,1)S(1)} collective-permute-done((bf16[256,128]{0,1:T(8,128)(2,1)S(1)}, bf16[256,128]{0,1:T(8,128)(2,1)S(1)}, u32[]{:S(2)}, u32[]{:S(2)}) %collective-permute-start.1) | collective-permute-done | bytes 65568 | tf_op jit(solution)/shard_map/ppermute | solution.py:16
  210.4 9.1 %collective-permute-done.2 = bf16[256,128]{0,1:T(8,128)(2,1)S(1)} collective-permute-done((bf16[256,128]{0,1:T(8,128)(2,1)S(1)}, bf16[256,128]{0,1:T(8,128)(2,1)S(1)}, u32[]{:S(2)}, u32[]{:S(2)}) %collective-permute-start.2) | collective-permute-done | bytes 65568 | tf_op jit(solution)/shard_map/ppermute | solution.py:16
  219.5 0.4 collective-permute-start.3
  219.9 8.4 %collective-permute-done.3 = bf16[256,128]{0,1:T(8,128)(2,1)S(1)} collective-permute-done((bf16[256,128]{0,1:T(8,128)(2,1)S(1)}, bf16[256,128]{0,1:T(8,128)(2,1)S(1)}, u32[]{:S(2)}, u32[]{:S(2)}) %collective-permute-start.3) | collective-permute-done | bytes 65568 | tf_op jit(solution)/shard_map/ppermute | solution.py:16
  228.5 3.9 convolution_convert_fusion
  232.4 0.8 reshape.239
  233.1 0.3 copy.70
  233.4 1.3 fusion.14
  234.7 2.0 slice_add_fusion
  236.7 17.3 %copy.85 = f32[8,256,256]{0,2,1:T(8,128)} copy(f32[8,256,256]{2,1,0:T(8,128)} %get-tuple-element.11) | data formatting | bytes 4194304 | tf_op jit(solution)/shard_map/reshape | solution.py:67
  253.9 16.2 %copy.86 = f32[8,256,256]{0,2,1:T(8,128)} copy(f32[8,256,256]{2,1,0:T(8,128)S(1)} %get-tuple-element.12) | data formatting | bytes 4194304 | tf_op jit(solution)/shard_map/reshape | solution.py:68
  270.1 16.0 %gather_fusion.6 = f32[2048,8]{1,0:T(8,128)S(1)} fusion(f32[8,65536]{0,1:T(8,128)} %bitcast.81, s32[2048]{0:T(1024)S(1)} %fusion.9), kind=kCustom, calls=%fused_computation.clone | custom fusion | bytes 139264 | tf_op jit(solution)/shard_map/jit(_take)/gather | solution.py:67
  286.2 16.0 %gather_fusion.7 = f32[2048,8]{1,0:T(8,128)S(1)} fusion(f32[8,65536]{0,1:T(8,128)} %bitcast.82, s32[2048]{0:T(1024)S(1)} %fusion.9), kind=kCustom, calls=%fused_computation.1.clone | custom fusion | bytes 139264 | tf_op jit(solution)/shard_map/jit(_take)/gather | solution.py:68
  302.2 0.3 broadcast_select_fusion.1
  302.6 1.5 maximum_bitcast_fusion.1
  304.1 0.7 add_compare_fusion
  304.8 2.3 gather_fusion.2
  307.1 301.9 %psum.7 = f32[8,256]{0,1:T(8,128)S(1)} all-reduce(f32[8,256]{0,1:T(8,128)S(1)} %bitcast.88), channel_id=1, replica_groups=mesh['tm'=64,'chan'=4] {'tm'}, use_global_device_ids=true, to_apply=%region_1.3 | all-reduce | flops 2048 | bytes 16384 | tf_op jit(solution)/shard_map/psum | solution.py:114
  609.0 59.1 %all_gather.7 = f32[32,256]{1,0:T(8,128)S(1)} all-gather(f32[8,256]{1,0:T(8,128)S(1)} %copy.78), channel_id=1, replica_groups=mesh['tm'=64,'chan'=4] {'chan'}, dimensions={0}, use_global_device_ids=true | all-gather | bytes 40960 | tf_op jit(solution)/shard_map/all_gather | solution.py:115
  668.1 0.6 gather_fusion.3
  668.7 0.8 slice_bitcast_fusion.3
  669.5 0.7 reshape.318
  670.1 3.4 all-to-all-start
  673.5 0.1 copy.79
  673.6 0.6 gather_fusion.5
  674.2 0.6 gather_fusion.4
  674.9 1.6 all-to-all-done
  676.5 0.5 broadcast.405
  677.0 0.7 reduce
  677.9 0.6 gather_fusion.1
  678.5 0.7 copy.83
  679.2 0.7 copy.84
  (49 shorter events, 0.8 us)
Async XLA Ops:
  7.2 25.5 %copy-start = (s32[32]{0:T(128)S(1)}, s32[32]{0:T(128)}, u32[]{:S(2)}) copy-start(s32[32]{0:T(128)} %param.11) | copy-start | bytes 388
  7.2 661.5 %reduce-scatter.2.cloned.1.call-start = ((), (), s32[]{:S(2)}) async-start(), calls=%async_computation.2 | async-start | bytes 2129920 | tf_op jit(solution)/shard_map/reduce_scatter | solution.py:103
  16.4 212.1 %collective-permute-start.7 = (bf16[256,128]{0,1:T(8,128)(2,1)S(1)}, bf16[256,128]{0,1:T(8,128)(2,1)S(1)}, u32[]{:S(2)}, u32[]{:S(2)}) collective-permute-start(bf16[256,128]{0,1:T(8,128)(2,1)S(1)} %copy.61), channel_id=1, source_target_pairs={{0,240},{4,244},{8,248},{12,252},{16,0},{20,4},{24,8},{28,12},{32,... | collective-permute-start | bytes 196616 | tf_op jit(solution)/shard_map/ppermute | solution.py:16
  22.8 205.7 %collective-permute-start.6 = (bf16[256,128]{0,1:T(8,128)(2,1)S(1)}, bf16[256,128]{0,1:T(8,128)(2,1)S(1)}, u32[]{:S(2)}, u32[]{:S(2)}) collective-permute-start(bf16[256,128]{0,1:T(8,128)(2,1)S(1)} %copy.61), channel_id=1, source_target_pairs={{0,244},{4,248},{8,252},{12,0},{16,4},{20,8},{24,12},{28,16},{32,2... | collective-permute-start | bytes 196616 | tf_op jit(solution)/shard_map/ppermute | solution.py:16
  24.0 204.4 %collective-permute-start.5 = (bf16[256,128]{0,1:T(8,128)(2,1)S(1)}, bf16[256,128]{0,1:T(8,128)(2,1)S(1)}, u32[]{:S(2)}, u32[]{:S(2)}) collective-permute-start(bf16[256,128]{0,1:T(8,128)(2,1)S(1)} %copy.61), channel_id=1, source_target_pairs={{0,248},{4,252},{8,0},{12,4},{16,8},{20,12},{24,16},{28,20},{32,24... | collective-permute-start | bytes 196616 | tf_op jit(solution)/shard_map/ppermute | solution.py:16
  29.5 198.8 %collective-permute-start.4 = (bf16[256,128]{0,1:T(8,128)(2,1)S(1)}, bf16[256,128]{0,1:T(8,128)(2,1)S(1)}, u32[]{:S(2)}, u32[]{:S(2)}) collective-permute-start(bf16[256,128]{0,1:T(8,128)(2,1)S(1)} %copy.61), channel_id=1, source_target_pairs={{0,252},{4,0},{8,4},{12,8},{16,12},{20,16},{24,20},{28,24},{32,28}... | collective-permute-start | bytes 196616 | tf_op jit(solution)/shard_map/ppermute | solution.py:16
  30.6 172.1 %collective-permute-start = (bf16[256,128]{0,1:T(8,128)(2,1)S(1)}, bf16[256,128]{0,1:T(8,128)(2,1)S(1)}, u32[]{:S(2)}, u32[]{:S(2)}) collective-permute-start(bf16[256,128]{0,1:T(8,128)(2,1)S(1)} %copy.61), channel_id=1, source_target_pairs={{0,16},{4,20},{8,24},{12,28},{16,32},{20,36},{24,40},{28,44},{32,4... | collective-permute-start | bytes 196616 | tf_op jit(solution)/shard_map/ppermute | solution.py:16
  202.7 7.6 %collective-permute-start.1 = (bf16[256,128]{0,1:T(8,128)(2,1)S(1)}, bf16[256,128]{0,1:T(8,128)(2,1)S(1)}, u32[]{:S(2)}, u32[]{:S(2)}) collective-permute-start(bf16[256,128]{0,1:T(8,128)(2,1)S(1)} %copy.61), channel_id=1, source_target_pairs={{0,12},{4,16},{8,20},{12,24},{16,28},{20,32},{24,36},{28,40},{32,4... | collective-permute-start | bytes 196616 | tf_op jit(solution)/shard_map/ppermute | solution.py:16
  210.4 9.1 %collective-permute-start.2 = (bf16[256,128]{0,1:T(8,128)(2,1)S(1)}, bf16[256,128]{0,1:T(8,128)(2,1)S(1)}, u32[]{:S(2)}, u32[]{:S(2)}) collective-permute-start(bf16[256,128]{0,1:T(8,128)(2,1)S(1)} %copy.61), channel_id=1, source_target_pairs={{0,8},{4,12},{8,16},{12,20},{16,24},{20,28},{24,32},{28,36},{32,40... | collective-permute-start | bytes 196616 | tf_op jit(solution)/shard_map/ppermute | solution.py:16
  219.5 8.8 %collective-permute-start.3 = (bf16[256,128]{0,1:T(8,128)(2,1)S(1)}, bf16[256,128]{0,1:T(8,128)(2,1)S(1)}, u32[]{:S(2)}, u32[]{:S(2)}) collective-permute-start(bf16[256,128]{0,1:T(8,128)(2,1)S(1)} %copy.61), channel_id=1, source_target_pairs={{0,4},{4,8},{8,12},{12,16},{16,20},{20,24},{24,28},{28,32},{32,36}... | collective-permute-start | bytes 196616 | tf_op jit(solution)/shard_map/ppermute | solution.py:16
  302.2 377.7 %copy-start.1 = (s32[32]{0:T(128)S(1)}, s32[32]{0:T(128)}, u32[]{:S(2)}) copy-start(s32[32]{0:T(128)} %param.11) | copy-start | bytes 388
  670.1 6.4 all-to-all-start
Sparse Core Ops, SparseCore 0:
  304.2 311.5 reduce-scatter.1
